TPU v7x, 256 devices: a whole 4x4x8 slice. The times are simulated.
256 devices in a mesh: group: 4 (over y), shard: 16 (over x_hi, z), tensor: 4 (over x_lo, core).
Axes of the slice: x: 4 (x_hi: 2, x_lo: 2; x = x_hi * 2 + x_lo), y: 4, z: 8, core: 2. Of those that a mesh axis runs over, the one named last changes fastest.
Arguments:
- group_weights: bfloat16 [4, 8, 1024, 8704], P('group', None, None, ('shard', 'tensor')), may hold values from -6 to 6
- anchor: float32 [8, 1024, 16, 4, 136], P(None, ('group', 'shard'), None, 'tensor'), may hold values from -6 to 6
- momentum: float32 [8, 1024, 16, 4, 136], P(None, ('group', 'shard'), None, 'tensor'), may hold values from -6 to 6
- group_embedding: bfloat16 [4, 32000, 1024], P('group', 'shard', 'tensor'), may hold values from -6 to 6
- emb_anchor: float32 [32000, 1024], P('shard', 'tensor'), may hold values from -6 to 6
- emb_momentum: float32 [32000, 1024], P('shard', 'tensor'), may hold values from -6 to 6
- basis: float32 [1024, 64], P('tensor'), may hold values from -0.1875 to 0.1875
Outputs:
- new_weights: bfloat16 [8, 1024, 8704], P(None, None, ('shard', 'tensor'))
- new_anchor: float32 [8, 1024, 16, 4, 136], P(None, ('group', 'shard'), None, 'tensor')
- new_momentum: float32 [8, 1024, 16, 4, 136], P(None, ('group', 'shard'), None, 'tensor')
- new_embedding: bfloat16 [32000, 1024], P('shard', 'tensor')
- new_emb_anchor: float32 [32000, 1024], P('shard', 'tensor')
- new_emb_momentum: float32 [32000, 1024], P('shard', 'tensor')
All inputs are finite; a program needn't handle non-finite values.
Results may differ from a plain program's by a relative error of at most 0.012.
Values may be sent and summed in bfloat16 or wider, within the bound.
No kernel may reach another device: no remote copies, remote signals or barrier semaphores. Data moves between devices by JAX's collectives and lax.ppermute only.
A program may use at most 128 MiB of HBM per device.

v0:
```python
import jax
import jax.numpy as jnp
from jax import lax
from jax.sharding import PartitionSpec as P

outer_rate = 0.7
momentum_decay = 0.9


def per_device(group_weights, anchor, momentum, group_embedding, emb_anchor, emb_momentum, basis):
    groups = lax.axis_size("group")
    layers = group_weights.shape[1]
    width = group_weights.shape[2]
    block = group_weights.shape[3]
    local_weights = group_weights[0]
    part = lax.psum_scatter(
        local_weights.astype(jnp.float32).astype(jnp.bfloat16),
        "group",
        scatter_dimension=1,
        tiled=True,
    )
    part = part.reshape(layers, part.shape[1], 1, 1, block)
    summed = lax.all_to_all(part, "shard", split_axis=1, concat_axis=2, tiled=True).astype(
        jnp.float32
    )
    delta = anchor - summed / groups
    moved = momentum_decay * momentum + delta
    stepped = anchor - outer_rate * (delta + momentum_decay * moved)
    stepped_half = stepped.astype(jnp.bfloat16)
    columns = lax.all_to_all(stepped_half, "shard", split_axis=2, concat_axis=1, tiled=True)
    whole = lax.all_gather(columns, "group", axis=1, tiled=True)
    new_weights = whole.reshape(layers, width, block)
    local_difference = emb_anchor - group_embedding[0].astype(jnp.float32)
    partial = jnp.dot(local_difference, basis, precision=lax.Precision.HIGHEST)
    coef = lax.psum(partial, ("group", "tensor")) * (1.0 / groups)
    emb_delta = jnp.dot(coef, basis.T, precision=lax.Precision.HIGHEST)
    emb_moved = momentum_decay * emb_momentum + emb_delta
    emb_stepped = emb_anchor - outer_rate * (emb_delta + momentum_decay * emb_moved)
    return (new_weights, stepped, moved, emb_stepped.astype(jnp.bfloat16), emb_stepped, emb_moved)


def solution(mesh):
    return jax.shard_map(
        per_device,
        mesh=mesh,
        in_specs=(
            P("group", None, None, ("shard", "tensor")),
            P(None, ("group", "shard"), None, "tensor", None),
            P(None, ("group", "shard"), None, "tensor", None),
            P("group", "shard", "tensor"),
            P("shard", "tensor"),
            P("shard", "tensor"),
            P("tensor", None),
        ),
        out_specs=(
            P(None, None, ("shard", "tensor")),
            P(None, ("group", "shard"), None, "tensor", None),
            P(None, ("group", "shard"), None, "tensor", None),
            P("shard", "tensor"),
            P("shard", "tensor"),
            P("shard", "tensor"),
        ),
        check_vma=False,
    )
```

profile of v0, /device:TPU:1, one launch (start us, length us, event | category | flops | bytes accessed | tf_op | source)
XLA Modules:
  0.0 275.6 jit_solution(16387879592642991854)
XLA Ops:
  8.0 0.0 copy-start
  8.0 0.0 reduce-scatter.2.cloned.1.call-start
  8.1 6.8 %copy.20 = bf16[1,8,1024,136]{3,1,2,0:T(8,128)(2,1)} copy(bf16[1,8,1024,136]{2,3,1,0:T(8,128)(2,1)} %param.7) | data formatting | bytes 4456448 | tf_op args[0]
  14.8 0.0 reduce-scatter.2.cloned.1.call-update
  14.8 53.3 %reduce-scatter.2.cloned.1.call-done = bf16[8,256,136]{2,0,1:T(8,128)(2,1)} async-done(((bf16[8,1024,136]{2,0,1:T(8,128)(2,1)}), bf16[8,256,136]{2,0,1:T(8,128)(2,1)}) %reduce-scatter.2.cloned.1.call-update) | async-done | bytes 557072 | tf_op jit(solution)/shard_map/reduce_scatter | solution.py:16
  68.1 35.6 %all_to_all.27 = bf16[8,256,1,1,136]{4,0,3,2,1:T(8,128)(2,1)S(1)} all-to-all(bf16[8,256,1,1,136]{4,0,3,2,1:T(8,128)(2,1)} %bitcast.25), channel_id=1, replica_groups=mesh['group'=4,'shard'=16,'tensor'=4] {'shard'}, dimensions={1} | all-to-all | bytes 1114112 | tf_op jit(solution)/shard_map/all_to_all | solution.py:23
  103.8 0.3 convert_multiply_fusion
  104.0 1.3 copy-done.2
  105.3 5.1 %fusion.8 = (bf16[8,16,16,1,136]{4,1,2,0,3:T(8,128)(2,1)S(1)}, f32[8,16,16,1,136]{4,1,2,0,3:T(8,128)}, f32[8,16,16,1,136]{4,1,2,0,3:T(8,128)S(1)}) fusion(f32[8,16,16,1,136]{4,3,2,1,0:T(1,128)S(1)} %copy-done.2, f32[8,16,16,1,136]{4,1,2,0,3:T(8,128)S(1)} %bitcast.21, f32[8,16,16,1,136]{4,3,2,1,0:T(1,128)S(1)} %copy-done.3), kind=kLoop, calls=%fused_computation.15 | loop fusion | flops 2228224 | bytes 6127616 | tf_op jit(solution)/shard_map/convert_element_type | solution.py:29
  110.4 1.1 copy.25
  111.5 6.4 %all-to-all-start.1 = ((bf16[8,16,16,1,136]{4,1,0,3,2:T(8,128)(2,1)}), bf16[8,16,16,1,136]{4,1,0,3,2:T(8,128)(2,1)S(1)}, u32[]{:S(2)}, u32[]{:S(2)}) async-start(bf16[8,16,16,1,136]{4,1,0,3,2:T(8,128)(2,1)} %copy.25), calls=%async_computation.2 | async-start | bytes 2097152 | tf_op jit(solution)/shard_map/all_to_all | solution.py:30
  117.9 0.0 all-reduce.2.cloned.1.call-start
  118.0 4.7 %fusion.1 = f32[2000,64]{0,1:T(8,128)} fusion(f32[256,64]{0,1:T(8,128)S(1)} %copy-done, f32[2000,256]{1,0:T(8,128)} %param.11, bf16[1,2000,256]{2,1,0:T(8,128)(2,1)} %param.10), kind=kOutput, calls=%fused_computation.5 | convolution fusion | flops 394240000 | bytes 3649536 | tf_op jit(solution)/shard_map/dot_general | solution.py:34
  122.7 0.0 all-reduce.2.cloned.1.call-update
  122.7 0.2 all-gather.2.cloned.1.call-start
  123.0 21.4 %all-to-all-done.1 = bf16[8,16,16,1,136]{4,1,0,3,2:T(8,128)(2,1)S(1)} async-done(((bf16[8,16,16,1,136]{4,1,0,3,2:T(8,128)(2,1)}), bf16[8,16,16,1,136]{4,1,0,3,2:T(8,128)(2,1)S(1)}, u32[]{:S(2)}, u32[]{:S(2)}) %all-to-all-start.1) | async-done | bytes 557088 | tf_op jit(solution)/shard_map/all_to_all | solution.py:30
  144.4 1.1 copy.26
  145.5 0.0 all-gather.2.cloned.1.call-update
  145.5 102.4 %all-reduce.2.cloned.1.call-done = f32[2000,64]{0,1:T(8,128)} async-done(((f32[2000,64]{0,1:T(8,128)}), f32[2000,64]{0,1:T(8,128)}) %all-reduce.2.cloned.1.call-update) | async-done | bytes 512016 | tf_op jit(solution)/shard_map/psum | solution.py:35
  247.9 7.0 %fusion.7 = (bf16[2000,256]{1,0:T(8,128)(2,1)}, f32[2000,256]{1,0:T(8,128)}, f32[2000,256]{1,0:T(8,128)}) fusion(f32[2000,256]{1,0:T(8,128)} %param.11, f32[2000,256]{1,0:T(8,128)} %param.12, f32[256,64]{0,1:T(8,128)S(1)} %copy-done, f32[2000,64]{0,1:T(8,128)} %all-reduce.2.cloned.1.call-done), kind=kOutput, calls=%fused_computation.14 | convolution fusion | flops 396928000 | bytes 9793536 | tf_op jit(solution)/shard_map/dot_general | solution.py:36
  254.8 0.0 copy-done.1
  254.8 3.7 %copy.28 = f32[8,16,16,1,136]{4,3,2,1,0:T(1,128)} copy(f32[8,16,16,1,136]{4,1,2,0,3:T(8,128)S(1)} %copy-done.1) | data formatting | bytes 2228224
  258.5 3.7 %copy.29 = f32[8,16,16,1,136]{4,3,2,1,0:T(1,128)} copy(f32[8,16,16,1,136]{4,1,2,0,3:T(8,128)S(1)} %get-tuple-element.23) | data formatting | bytes 2228224
  262.3 5.9 %copy.27 = bf16[8,1024,136]{1,2,0:T(8,128)(2,1)} copy(bf16[8,1024,136]{2,1,0:T(8,128)(2,1)} %bitcast.22) | data formatting | bytes 4456448
  (6 shorter events, 0.0 us)
Async XLA Ops:
  8.0 110.0 %copy-start = (f32[256,64]{0,1:T(8,128)S(1)}, f32[256,64]{0,1:T(8,128)}, u32[]{:S(2)}) copy-start(f32[256,64]{0,1:T(8,128)} %param.13) | copy-start | bytes 196612
  8.0 60.1 %reduce-scatter.2.cloned.1.call-start = ((), (), s32[]{:S(2)}) async-start(), calls=%async_computation.3 | async-start | bytes 5242880 | tf_op jit(solution)/shard_map/reduce_scatter | solution.py:16
  68.1 35.9 %copy-start.3 = (f32[8,16,16,1,136]{4,3,2,1,0:T(1,128)S(1)}, f32[8,16,16,1,136]{4,3,2,1,0:T(1,128)}, u32[]{:S(2)}) copy-start(f32[8,16,16,1,136]{4,3,2,1,0:T(1,128)} %param.8) | copy-start | bytes 3342340
  103.8 1.6 copy-start.2
  111.5 32.9 %all-to-all-start.1 = ((bf16[8,16,16,1,136]{4,1,0,3,2:T(8,128)(2,1)}), bf16[8,16,16,1,136]{4,1,0,3,2:T(8,128)(2,1)S(1)}, u32[]{:S(2)}, u32[]{:S(2)}) async-start(bf16[8,16,16,1,136]{4,1,0,3,2:T(8,128)(2,1)} %copy.25), calls=%async_computation.2 | async-start | bytes 2097152 | tf_op jit(solution)/shard_map/all_to_all | solution.py:30
  117.9 129.9 %all-reduce.2.cloned.1.call-start = ((), (), s32[]{:S(2)}) async-start(), calls=%async_computation.5 | async-start | bytes 1048576 | tf_op jit(solution)/shard_map/psum | solution.py:35
  122.7 139.5 %all-gather.2.cloned.1.call-start = ((), (), s32[]{:S(2)}) async-start(), calls=%async_computation.4 | async-start | bytes 5242880 | tf_op jit(solution)/shard_map/all_gather | solution.py:31
  247.9 7.0 %copy-start.1 = (f32[8,16,16,1,136]{4,1,2,0,3:T(8,128)S(1)}, f32[8,16,16,1,136]{4,1,2,0,3:T(8,128)}, u32[]{:S(2)}) copy-start(f32[8,16,16,1,136]{4,1,2,0,3:T(8,128)} %get-tuple-element.22) | copy-start | bytes 3342340
Sparse Core Ops, SparseCore 0:
  15.0 53.1 reduce-scatter.1
  145.6 49.0 all-gather.1
Sparse Core Ops, SparseCore 1:
  122.8 125.0 all-reduce.1
where the time goes:
time: 276 us
  waiting for transfers between devices  177 us (64%)
  blocking collectives  35.6 us (13%)
  local copies, waits for them, and re-layouts  23.6 us (9%)
  between operations  15.5 us (6%)
  matrix products  11.7 us (4%)
  starting transfers between devices  6.68 us (2%)
  other arithmetic  5.36 us (2%)
    psum x1, waiting for transfers between devices, per_device(): coef = lax.psum(partial, ('group', 'tensor')) * (1.0 / groups)  102 us
    reduce_scatter x1, waiting for transfers between devices, per_device(): lax.psum_scatter(local_weights.astype(jnp.float32).astype(jnp.bfloat16),...  53.3 us
    all_to_all x1, blocking collectives, per_device(): lax.all_to_all(part, 'shard', split_axis=1, concat_axis=2, tiled=True)  35.6 us
    all_to_all x1, waiting for transfers between devices, per_device(): lax.all_to_all(stepped_half, 'shard', split_axis=2, concat_axis=1, tiled=...  21.4 us
    unnamed x12, local copies, waits for them, and re-layouts  21.4 us
    dot_general x1, matrix products, per_device(): emb_delta = jnp.dot(coef, basis.T, precision=lax.Precision.HIGHEST)  6.95 us
    all_to_all x1, starting transfers between devices, per_device(): lax.all_to_all(stepped_half, 'shard', split_axis=2, concat_axis=1, tiled=...  6.37 us
  transfers between devices with their start and end apart: 4, of which 3 were waited for; matrix products, arithmetic and copies ran while one was open for 7% of the time, Pallas kernels for 0%

commit v1 on v0

--- a/solution.py
+++ b/solution.py
@@ -32,7 +32,7 @@
     new_weights = whole.reshape(layers, width, block)
     local_difference = emb_anchor - group_embedding[0].astype(jnp.float32)
     partial = jnp.dot(local_difference, basis, precision=lax.Precision.HIGHEST)
-    coef = lax.psum(partial, ("group", "tensor")) * (1.0 / groups)
+    coef = jnp.sum(lax.all_gather(partial, ("group", "tensor")), axis=0) * (1.0 / groups)
     emb_delta = jnp.dot(coef, basis.T, precision=lax.Precision.HIGHEST)
     emb_moved = momentum_decay * emb_momentum + emb_delta
     emb_stepped = emb_anchor - outer_rate * (emb_delta + momentum_decay * emb_moved)

time: 276 us -> 266 us (0.964)
  waiting for transfers between devices: 177 us -> 140 us
  blocking collectives: 35.6 us -> 67.3 us
  starting transfers between devices: 6.68 us -> 0.3 us
  other arithmetic: 5.36 us -> 9.32 us
    psum x1 -> x0, waiting for transfers between devices: 102 us -> none  [per_device(): coef = lax.psum(partial, ('group', 'tensor')) * (1.0 / groups)]
    all_gather x0 -> x1, waiting for transfers between devices: none -> 52.1 us  [per_device(): lax.all_gather(partial, ('group', 'tensor'))]
    all_gather x1, waiting for transfers between devices: 0.01 us -> 34.9 us  [per_device(): whole = lax.all_gather(columns, 'group', axis=1, tiled=True)]
    all_to_all x0 -> x1, blocking collectives: none -> 31.7 us  [per_device(): lax.all_to_all(stepped_half, 'shard', split_axis=2, concat_axis=1, tiled=...]
    all_to_all x1 -> x0, waiting for transfers between devices: 21.4 us -> none  [per_device(): lax.all_to_all(stepped_half, 'shard', split_axis=2, concat_axis=1, tiled=...]
    all_to_all x1 -> x0, starting transfers between devices: 6.37 us -> none  [per_device(): lax.all_to_all(stepped_half, 'shard', split_axis=2, concat_axis=1, tiled=...]
    reduce_sum x0 -> x1, other arithmetic: none -> 3.96 us  [per_device(): jnp.sum(lax.all_gather(partial, ('group', 'tensor')), axis=0)]
    unnamed x12 -> x14, local copies, waits for them, and re-layouts: 21.4 us -> 23 us
  transfers between devices with their start and end apart: 4 -> 3, of which waited for: 3 -> 3; matrix products, arithmetic and copies ran while one was open for 7% -> 7% of each run, Pallas kernels for 0% -> 0%
where the time goes in v1:
time: 266 us
  waiting for transfers between devices  140 us (53%)
  blocking collectives  67.3 us (25%)
  local copies, waits for them, and re-layouts  24.2 us (9%)
  between operations  13.8 us (5%)
  matrix products  10.5 us (4%)
  other arithmetic  9.32 us (4%)
    reduce_scatter x1, waiting for transfers between devices, per_device(): lax.psum_scatter(local_weights.astype(jnp.float32).astype(jnp.bfloat16),...  53.2 us
    all_gather x1, waiting for transfers between devices, per_device(): lax.all_gather(partial, ('group', 'tensor'))  52.1 us
    all_to_all x1, blocking collectives, per_device(): lax.all_to_all(part, 'shard', split_axis=1, concat_axis=2, tiled=True)  35.6 us
    all_gather x1, waiting for transfers between devices, per_device(): whole = lax.all_gather(columns, 'group', axis=1, tiled=True)  34.9 us
    all_to_all x1, blocking collectives, per_device(): lax.all_to_all(stepped_half, 'shard', split_axis=2, concat_axis=1, tiled=...  31.7 us
    unnamed x14, local copies, waits for them, and re-layouts  23 us
    dot_general x1, matrix products, per_device(): emb_delta = jnp.dot(coef, basis.T, precision=lax.Precision.HIGHEST)  6.03 us
  transfers between devices with their start and end apart: 3, of which 3 were waited for; matrix products, arithmetic and copies ran while one was open for 7% of the time, Pallas kernels for 0%

profile of v1, /device:TPU:1, one launch (start us, length us, event | category | flops | bytes accessed | tf_op | source)
XLA Modules:
  0.0 265.8 jit_solution(14110124731400412284)
XLA Ops:
  7.2 0.0 reduce-scatter.2.cloned.1.call-start
  7.2 6.8 %copy.20 = bf16[1,8,1024,136]{3,1,2,0:T(8,128)(2,1)} copy(bf16[1,8,1024,136]{2,3,1,0:T(8,128)(2,1)} %param.7) | data formatting | bytes 4456448 | tf_op args[0]
  14.0 0.0 reduce-scatter.2.cloned.1.call-update
  14.0 0.0 all-gather.5.cloned.1.call-start
  14.1 53.2 %reduce-scatter.2.cloned.1.call-done = bf16[8,256,136]{2,0,1:T(8,128)(2,1)} async-done(((bf16[8,1024,136]{2,0,1:T(8,128)(2,1)}), bf16[8,256,136]{2,0,1:T(8,128)(2,1)}) %reduce-scatter.2.cloned.1.call-update) | async-done | bytes 557072 | tf_op jit(solution)/shard_map/reduce_scatter | solution.py:16
  67.3 35.6 %all_to_all.27 = bf16[8,256,1,1,136]{4,0,3,2,1:T(8,128)(2,1)S(1)} all-to-all(bf16[8,256,1,1,136]{4,0,3,2,1:T(8,128)(2,1)} %bitcast.27), channel_id=1, replica_groups=mesh['group'=4,'shard'=16,'tensor'=4] {'shard'}, dimensions={1} | all-to-all | bytes 1114112 | tf_op jit(solution)/shard_map/all_to_all | solution.py:23
  102.9 0.3 convert_multiply_fusion
  103.2 1.3 copy-done.2
  104.5 5.1 %fusion.7 = (bf16[8,16,16,1,136]{4,1,2,0,3:T(8,128)(2,1)S(1)}, f32[8,16,16,1,136]{4,1,2,0,3:T(8,128)}, f32[8,16,16,1,136]{4,1,2,0,3:T(8,128)S(1)}) fusion(f32[8,16,16,1,136]{4,3,2,1,0:T(1,128)S(1)} %copy-done.2, f32[8,16,16,1,136]{4,1,2,0,3:T(8,128)S(1)} %bitcast.23, f32[8,16,16,1,136]{4,3,2,1,0:T(1,128)S(1)} %copy-done.3), kind=kLoop, calls=%fused_computation.15 | loop fusion | flops 2228224 | bytes 6127616 | tf_op jit(solution)/shard_map/convert_element_type | solution.py:29
  109.6 0.1 copy.25
  109.7 31.7 %all_to_all.28 = bf16[8,16,16,1,136]{4,1,0,3,2:T(8,128)(2,1)S(1)} all-to-all(bf16[8,16,16,1,136]{4,1,0,3,2:T(8,128)(2,1)S(1)} %copy.25), channel_id=1, replica_groups=mesh['group'=4,'shard'=16,'tensor'=4] {'shard'}, dimensions={2} | all-to-all | bytes 1114112 | tf_op jit(solution)/shard_map/all_to_all | solution.py:30
  141.4 1.1 copy.26
  142.5 0.0 all-gather.5.cloned.1.call-update
  142.5 0.2 all-gather.7.cloned.1.call-start
  142.8 0.3 copy-done.4
  143.0 4.5 %convolution_bitcast_fusion = f32[1,2000,64]{1,2,0:T(8,128)} fusion(f32[256,64]{0,1:T(8,128)S(1)} %copy-done, f32[2000,256]{1,0:T(8,128)} %param.11, bf16[1,2000,256]{2,1,0:T(8,128)(2,1)S(1)} %copy-done.4), kind=kOutput, calls=%fused_computation | convolution fusion | flops 394240000 | bytes 3649536 | tf_op jit(solution)/shard_map/dot_general | solution.py:34
  147.5 0.0 all-gather.7.cloned.1.call-update
  147.5 5.1 %copy.28 = f32[8,16,16,1,136]{4,3,2,1,0:T(1,128)} copy(f32[8,16,16,1,136]{4,1,2,0,3:T(8,128)} %get-tuple-element.22) | data formatting | bytes 2228224
  152.6 3.7 %copy.29 = f32[8,16,16,1,136]{4,3,2,1,0:T(1,128)} copy(f32[8,16,16,1,136]{4,1,2,0,3:T(8,128)S(1)} %get-tuple-element.23) | data formatting | bytes 2228224
  156.3 34.9 %all-gather.5.cloned.1.call-done = bf16[8,1024,1,1,136]{4,1,0,3,2:T(8,128)(2,1)} async-done(((bf16[8,256,1,1,136]{4,1,0,3,2:T(8,128)(2,1)}), bf16[8,1024,1,1,136]{4,1,0,3,2:T(8,128)(2,1)}) %all-gather.5.cloned.1.call-update) | async-done | bytes 2228240 | tf_op jit(solution)/shard_map/all_gather | solution.py:31
  191.3 5.9 %copy.27 = bf16[8,1024,136]{1,2,0:T(8,128)(2,1)} copy(bf16[8,1024,136]{2,1,0:T(8,128)(2,1)} %bitcast.24) | data formatting | bytes 4456448
  197.1 52.1 %all-gather.7.cloned.1.call-done = f32[16,2000,64]{1,2,0:T(8,128)} async-done(((f32[1,2000,64]{1,2,0:T(8,128)}), f32[16,2000,64]{1,2,0:T(8,128)}) %all-gather.7.cloned.1.call-update) | async-done | bytes 8192016 | tf_op jit(solution)/shard_map/all_gather | solution.py:35
  249.2 4.0 %reduce_sum.9 = f32[2000,64]{0,1:T(8,128)S(1)} reduce(f32[16,2000,64]{1,2,0:T(8,128)} %all-gather.7.cloned.1.call-done, f32[]{:T(128)} %constant.1.clone.1), dimensions={0}, to_apply=%region_1.0 | reduce | flops 1920000 | bytes 8704004 | tf_op jit(solution)/shard_map/reduce_sum | solution.py:35
  253.2 6.0 %fusion.6 = (bf16[2000,256]{1,0:T(8,128)(2,1)}, f32[2000,256]{1,0:T(8,128)}, f32[2000,256]{1,0:T(8,128)}) fusion(f32[2000,256]{1,0:T(8,128)S(1)} %copy-done.1, f32[2000,256]{1,0:T(8,128)} %param.12, f32[256,64]{0,1:T(8,128)S(1)} %copy-done, f32[2000,64]{0,1:T(8,128)S(1)} %reduce_sum.9), kind=kOutput, calls=%fused_computation.14 | convolution fusion | flops 396928000 | bytes 9793536 | tf_op jit(solution)/shard_map/dot_general | solution.py:36
  (8 shorter events, 0.0 us)
Async XLA Ops:
  7.2 135.6 %copy-start = (f32[256,64]{0,1:T(8,128)S(1)}, f32[256,64]{0,1:T(8,128)}, u32[]{:S(2)}) copy-start(f32[256,64]{0,1:T(8,128)} %param.13) | copy-start | bytes 196612
  7.2 60.1 %reduce-scatter.2.cloned.1.call-start = ((), (), s32[]{:S(2)}) async-start(), calls=%async_computation.3 | async-start | bytes 5242880 | tf_op jit(solution)/shard_map/reduce_scatter | solution.py:16
  14.0 177.2 %all-gather.5.cloned.1.call-start = ((), (), s32[]{:S(2)}) async-start(), calls=%async_computation.4 | async-start | bytes 5242880 | tf_op jit(solution)/shard_map/all_gather | solution.py:31
  67.3 35.9 %copy-start.3 = (f32[8,16,16,1,136]{4,3,2,1,0:T(1,128)S(1)}, f32[8,16,16,1,136]{4,3,2,1,0:T(1,128)}, u32[]{:S(2)}) copy-start(f32[8,16,16,1,136]{4,3,2,1,0:T(1,128)} %param.8) | copy-start | bytes 3342340
  102.9 1.6 copy-start.2
  141.4 1.6 copy-start.4
  142.5 106.7 %all-gather.7.cloned.1.call-start = ((), (), s32[]{:S(2)}) async-start(), calls=%async_computation.5 | async-start | bytes 8912896 | tf_op jit(solution)/shard_map/all_gather | solution.py:35
  197.1 56.1 %copy-start.1 = (f32[2000,256]{1,0:T(8,128)S(1)}, f32[2000,256]{1,0:T(8,128)}, u32[]{:S(2)}) copy-start(f32[2000,256]{1,0:T(8,128)} %param.11) | copy-start | bytes 6144004
Sparse Core Ops, SparseCore 0:
  14.1 53.1 reduce-scatter.1
  142.7 48.5 all-gather.4
  193.7 55.4 all-gather.6
